TPU v7x, 128 devices: a whole 4x4x4 slice. The times are simulated.
128 devices in a mesh: pix: 8 (over y_hi, z), tm: 16 (over x, y_lo, core).
Axes of the slice: x: 4, y: 4 (y_hi: 2, y_lo: 2; y = y_hi * 2 + y_lo), z: 4, core: 2. Of those that a mesh axis runs over, the one named last changes fastest.
Arguments:
- frames: float32 [16, 192, 12288], P('tm', 'pix'), may hold values from 0.05 to 5
- pixel_order: int32 [12288], replicated, may hold values from 0 to 12287, each once
- cycle_sizes: int32 [64], replicated, may hold values from 1 to 384, 12288 in all
- kernel: float32 [5], replicated, may hold values from 0.1 to 1
Outputs:
- correlation: float32 [64, 3072, 3072], P('pix', 'tm')
Inputs may be any that keep to these rules, and one draw needn't show every extreme that they name: `cycle_sizes`: every cycle has one or more pixels, the sizes sum to 12288, and one cycle has exactly 384.
All inputs are finite; a program needn't handle non-finite values.
Results may differ from a plain program's by a relative error of at most 0.00005.
Values sent between devices are 32-bit elements; how exact they have to be, the bound alone decides.
No kernel may reach another device: no remote copies, remote signals or barrier semaphores. Data moves between devices by JAX's collectives and lax.ppermute only.
A program may use at most 256 MiB of HBM per device.

v0:
```python
import jax
import jax.numpy as jnp
from jax import lax
from jax.sharding import Mesh
from jax.sharding import PartitionSpec as P

REACH = 2
PIX = ("yh", "z")
TM = ("x", "yl", "c")
CHIPS = ("x", "yl")


def halo_frames(block, width):
    count = lax.axis_size(TM)
    forward = [(i, i + 1) for i in range(count - 1)]
    backward = [(i + 1, i) for i in range(count - 1)]
    n = block.shape[-1]
    low = lax.ppermute(block[..., n - width :], TM, forward)
    high = lax.ppermute(block[..., :width], TM, backward)
    return jnp.concatenate([low, block, high], axis=-1)


def correlate(left, right):
    return jnp.einsum(
        "rfs,rgs->rfg",
        left,
        right,
        precision=lax.Precision.HIGH,
        preferred_element_type=jnp.float32,
    )


def per_device(frames, pixel_order, cycle_sizes, kernel):
    block = frames[0]
    sub, pixels = block.shape
    cycles = cycle_sizes.shape[0]
    cap = 2 * pixels // cycles
    groups = lax.axis_size(PIX)
    owned = cycles // groups
    half = owned // 2
    window = owned * cap
    starts = (jnp.cumsum(cycle_sizes) - cycle_sizes).astype(jnp.int32)
    me = lax.axis_index(PIX)
    ordered = jnp.take(block.T, pixel_order, axis=0)
    ordered = jnp.pad(ordered, ((0, window), (0, 0)))
    chunks = jnp.stack(
        [lax.dynamic_slice_in_dim(ordered, starts[d * owned], window, 0) for d in range(groups)]
    )
    got = lax.all_to_all(chunks, PIX, 0, 0, tiled=True)
    got = jnp.pad(got, ((0, 0), (0, cap), (0, 0)))
    base = starts[me * owned]
    slots = jnp.arange(cap, dtype=jnp.int32)
    picked = []
    for l in range(owned):
        r = me * owned + l
        rows = lax.dynamic_slice_in_dim(got, starts[r] - base, cap, 1)
        picked.append(jnp.where((slots < cycle_sizes[r])[None, :, None], rows, 0.0))
    picked = jnp.stack(picked)
    picked = jnp.transpose(picked, (0, 2, 1, 3)).reshape(owned, cap, groups * sub)
    tblk = groups * sub
    total = jnp.sum(picked, axis=1, keepdims=True)
    scaled = picked / total
    rimmed = halo_frames(scaled, REACH)
    smooth = kernel[0] * rimmed[..., 0:tblk]
    for shift_step in range(1, 2 * REACH + 1):
        smooth = smooth + kernel[shift_step] * rimmed[..., shift_step : shift_step + tblk]
    smooth = jnp.swapaxes(smooth, 1, 2)
    core = lax.axis_index("c")
    keep = lax.dynamic_slice_in_dim(smooth, core * half, half, 0)
    give = lax.dynamic_slice_in_dim(smooth, (1 - core) * half, half, 0)
    other = lax.ppermute(give, "c", [(0, 1), (1, 0)])
    pair = jnp.where(
        core == 0, jnp.concatenate([keep, other], 1), jnp.concatenate([other, keep], 1)
    )
    right = lax.all_gather(pair, CHIPS, axis=1, tiled=True)
    scale = lax.dynamic_slice_in_dim(cycle_sizes, me * owned + core * half, half).astype(
        jnp.float32
    )
    scale = scale[:, None, None]
    sent = correlate(other * scale, right)
    back = lax.ppermute(sent, "c", [(0, 1), (1, 0)])
    mine = correlate(keep * scale, right)
    return jnp.where(core == 0, jnp.concatenate([mine, back], 0), jnp.concatenate([back, mine], 0))


def solution(mesh):
    pix, tm = (mesh.shape["pix"], mesh.shape["tm"])
    fine = Mesh(mesh.devices.reshape(2, pix // 2, tm // 4, 2, 2), PIX + TM)
    placed = (P(TM, PIX, None), P(), P(), P())
    return jax.shard_map(
        per_device, mesh=fine, in_specs=placed, out_specs=P(PIX, TM, None), check_vma=False
    )
```

profile of v0, /device:TPU:1, one launch (start us, length us, event | category | flops | bytes accessed | tf_op | source)
XLA Modules:
  0.0 593.9 jit_solution(16584004930738798835)
XLA Ops:
  8.2 1.7 fusion.42
  21.5 4.9 copy.7
  31.3 43.9 %gather_fusion = f32[12288,24]{1,0:T(8,128)} fusion(f32[12288,24]{1,0:T(8,128)} %bitcast.91, s32[12288]{0:T(1024)S(1)} %fusion.39), kind=kCustom, calls=%fused_computation | custom fusion | bytes 2408448 | tf_op jit(solution)/shard_map/jit(_take)/gather | solution.py:44
  75.2 8.6 %broadcast_select_fusion = f32[12288,24]{1,0:T(8,128)S(1)} fusion(f32[12288,24]{1,0:T(8,128)} %gather_fusion, pred[12288]{0:T(1024)(128)(4,1)S(1)} %compare_and_fusion), kind=kLoop, calls=%fused_computation.10 | loop fusion | flops 294912 | bytes 2371584 | tf_op jit(solution)/shard_map/jit(_take)/select_n | solution.py:44
  83.8 7.3 %pad_dynamic-slice_fusion = (f32[3072,24]{1,0:T(8,128)}, f32[3072,24]{1,0:T(8,128)}, f32[3072,24]{1,0:T(8,128)}, f32[3072,24]{1,0:T(8,128)}, f32[3072,24]{1,0:T(...) fusion(s32[]{:T(128)S(6)} %select_n.149, f32[12288,24]{1,0:T(8,128)S(1)} %broadcast_select_fusion, ...), kind=kLoop, calls=%fused_computation.2 | loop fusion | bytes 3538976 | tf_op jit(solution)/shard_map/dynamic_slice | solution.py:47
  91.1 2.0 copy.16
  93.1 2.6 copy.10
  98.0 2.7 copy.13
  100.7 2.6 copy.14
  105.6 1.7 bitcast_dynamic-update-slice_fusion.7
  107.3 1.7 bitcast_dynamic-update-slice_fusion.6
  113.4 8.5 %all-to-all-start = ((f32[8,3072,24]{1,2,0:T(8,128)}), f32[8,3072,24]{1,2,0:T(8,128)S(1)}, u32[]{:S(2)}, u32[]{:S(2)}) async-start(f32[8,3072,24]{1,2,0:T(8,128)} %bitcast_dynamic-update-slice_fusion), calls=%async_computation | async-start | bytes 4718592 | tf_op jit(solution)/shard_map/all_to_all | solution.py:49
  135.7 15.2 %all-to-all-done = f32[8,3072,24]{1,2,0:T(8,128)S(1)} async-done(((f32[8,3072,24]{1,2,0:T(8,128)}), f32[8,3072,24]{1,2,0:T(8,128)S(1)}, u32[]{:S(2)}, u32[]{:S(2)}) %all-to-all-start) | async-done | bytes 2359328 | tf_op jit(solution)/shard_map/all_to_all | solution.py:49
  153.8 2.0 bitcast_divide_fusion
  155.8 3.4 collective-permute-start
  159.2 1.9 collective-permute-start.1
  161.8 2.5 collective-permute-done.1
  164.3 4.7 fusion.3
  169.5 2.8 collective-permute-done.2
  172.3 1.6 maximum_select_fusion.1
  174.6 364.7 %all-gather.2.cloned.1.call-done = f32[4,3072,384]{2,1,0:T(8,128)} async-done(((f32[4,384,384]{2,1,0:T(8,128)}), f32[4,3072,384]{2,1,0:T(8,128)}) %all-gather.2.cloned.1.call-update) | async-done | bytes 18874384 | tf_op jit(solution)/shard_map/all_gather | solution.py:75
  539.3 16.5 %fusion.10 = f32[4,192,3072]{2,1,0:T(8,128)} fusion(f32[4,3072,384]{2,1,0:T(8,128)} %all-gather.2.cloned.1.call-done, f32[4,192,384]{2,1,0:T(8,128)S(1)} %collective-permute-done.2, f32[4]{0:T(128)S(1)} %dynamic-slice_convert_fusion), kind=kOutput, calls=%fused_computation.37 | convolution fusion | flops 5436112896 | bytes 29491216 | tf_op jit(solution)/shard_map/rfs,rgs->rfg/dot_general | solution.py:24
  556.7 13.6 %fusion.12 = f32[4,192,3072]{2,1,0:T(8,128)S(1)} fusion(f32[4,3072,384]{2,1,0:T(8,128)} %all-gather.2.cloned.1.call-done, f32[4,192,384]{2,1,0:T(8,128)S(1)} %get-tuple-element.13, f32[4]{0:T(128)S(1)} %dynamic-slice_convert_fusion), kind=kOutput, calls=%fused_computation.40 | convolution fusion | flops 5436112896 | bytes 29491216 | tf_op jit(solution)/shard_map/rfs,rgs->rfg/dot_general | solution.py:24
  571.3 15.7 %maximum_select_fusion = f32[8,192,3072]{2,1,0:T(8,128)} fusion(f32[4,192,3072]{2,1,0:T(8,128)} %collective-permute-done.3, f32[4,192,3072]{2,1,0:T(8,128)S(1)} %fusion.12, pred[]{:T(512)S(6)} %eq.4), kind=kLoop, calls=%fused_computation.1 | loop fusion | flops 14155776 | bytes 37748736 | tf_op jit(solution)/shard_map/jit(_where)/select_n | solution.py:83
  (68 shorter events, 23.9 us)
Async XLA Ops:
  91.1 4.6 copy-start.4
  91.1 5.8 copy-start.3
  96.8 6.4 %copy-start.2 = (f32[3072,24]{1,0:T(8,128)S(1)}, f32[3072,24]{1,0:T(8,128)}, u32[]{:S(2)}) copy-start(f32[3072,24]{1,0:T(8,128)} %get-tuple-element.11) | copy-start | bytes 884740
  98.0 6.4 %copy-start.1 = (f32[3072,24]{1,0:T(8,128)S(1)}, f32[3072,24]{1,0:T(8,128)}, u32[]{:S(2)}) copy-start(f32[3072,24]{1,0:T(8,128)} %get-tuple-element.12) | copy-start | bytes 884740
  104.4 4.6 copy-start.9
  104.4 5.3 copy-start.8
  104.4 6.0 %copy-start.7 = (f32[3072,24]{0,1:T(8,128)S(1)}, f32[3072,24]{0,1:T(8,128)}, u32[]{:S(2)}) copy-start(f32[3072,24]{0,1:T(8,128)} %copy.13) | copy-start | bytes 884740
  104.4 6.8 %copy-start.6 = (f32[3072,24]{0,1:T(8,128)S(1)}, f32[3072,24]{0,1:T(8,128)}, u32[]{:S(2)}) copy-start(f32[3072,24]{0,1:T(8,128)} %copy.14) | copy-start | bytes 884740
  104.4 7.5 %copy-start.5 = (f32[3072,24]{0,1:T(8,128)S(1)}, f32[3072,24]{0,1:T(8,128)}, u32[]{:S(2)}) copy-start(f32[3072,24]{0,1:T(8,128)} %copy.15) | copy-start | bytes 884740
  113.4 37.5 %all-to-all-start = ((f32[8,3072,24]{1,2,0:T(8,128)}), f32[8,3072,24]{1,2,0:T(8,128)S(1)}, u32[]{:S(2)}, u32[]{:S(2)}) async-start(f32[8,3072,24]{1,2,0:T(8,128)} %bitcast_dynamic-update-slice_fusion), calls=%async_computation | async-start | bytes 4718592 | tf_op jit(solution)/shard_map/all_to_all | solution.py:49
  121.9 417.4 %all-gather.2.cloned.1.call-start = ((), (), s32[]{:S(2)}) async-start(), calls=%async_computation.1 | async-start | bytes 21233664 | tf_op jit(solution)/shard_map/all_gather | solution.py:75
  152.1 1.4 copy-start
  153.8 7.3 %copy-start.11 = (f32[5]{0:T(128)S(1)}, f32[5]{0:T(128)}, u32[]{:S(2)}) copy-start(f32[5]{0:T(128)} %param.7) | copy-start | bytes 64
  155.8 6.0 %collective-permute-start = (f32[8,384,2]{1,2,0:T(2,128)S(1)}, f32[8,384,2]{1,2,0:T(2,128)S(1)}, u32[]{:S(2)}, u32[]{:S(2)}) collective-permute-start(f32[8,384,2]{1,2,0:T(2,128)S(1)} %get-tuple-element.15), channel_id=1, source_target_pairs={{0,1},{1,2},{2,3},{3,4},{4,5},{5,6},{6,7},{7,8},{8,9},{9,10},{10,1... | collective-permute-start | bytes 73736 | tf_op jit(solution)/shard_map/ppermute | solution.py:18
  159.2 5.1 collective-permute-start.1
  169.2 3.1 collective-permute-start.2
  173.9 0.7 copy-start.10
  555.8 15.5 %collective-permute-start.3 = (f32[4,192,3072]{2,1,0:T(8,128)}, f32[4,192,3072]{2,1,0:T(8,128)}, u32[]{:S(2)}, u32[]{:S(2)}) collective-permute-start(f32[4,192,3072]{2,1,0:T(8,128)} %fusion.10), channel_id=1, source_target_pairs={{0,1},{1,0},{2,3},{3,2},{4,5},{5,4},{6,7},{7,6},{8,9},{9,8},{10,11... | collective-permute-start | bytes 28311560 | tf_op jit(solution)/shard_map/ppermute | solution.py:81
Sparse Core Ops, SparseCore 0:
  174.0 365.2 all-gather.1
where the time goes:
time: 595 us; the launch traced here: 594 us
  waiting for transfers between devices  386 us (65%)
  local copies, waits for them, and re-layouts  83.7 us (14%)
  other arithmetic  41.4 us (7%)
  between operations  37.4 us (6%)
  matrix products  30.1 us (5%)
  starting transfers between devices  14.9 us (3%)
    all_gather x1, waiting for transfers between devices, per_device(): right = lax.all_gather(pair, CHIPS, axis=1, tiled=True)  365 us
    gather x1, local copies, waits for them, and re-layouts, per_device(): ordered = jnp.take(block.T, pixel_order, axis=0)  43.9 us
    dot_general x2, matrix products, correlate(): jnp.einsum('rfs,rgs->rfg', left, right, precision=lax.Precision.HIGH, pre...  30.1 us
    dynamic_slice x9, local copies, waits for them, and re-layouts, per_device(): lax.dynamic_slice_in_dim(ordered, starts[d * owned], window, 0)  21.8 us
    select_n x1, other arithmetic, per_device(): jnp.where(core == 0, jnp.concatenate([mine, back], 0), jnp.concatenate([b...  15.7 us
    all_to_all x1, waiting for transfers between devices, per_device(): got = lax.all_to_all(chunks, PIX, 0, 0, tiled=True)  15.2 us
    unnamed x32, local copies, waits for them, and re-layouts  14 us
  transfers between devices with their start and end apart: 6, of which 5 were waited for; matrix products, arithmetic and copies ran while one was open for 3% of the time, Pallas kernels for 0%

commit v1 on v0

--- a/solution.py
+++ b/solution.py
@@ -72,7 +72,19 @@
     pair = jnp.where(
         core == 0, jnp.concatenate([keep, other], 1), jnp.concatenate([other, keep], 1)
     )
-    right = lax.all_gather(pair, CHIPS, axis=1, tiled=True)
+
+    def drive_the_racks(payload, axis_key, axis_no):
+        return jnp.concatenate(
+            lax.all_to_all(
+                jnp.stack(lax.axis_size(axis_key) * [payload], axis=0),
+                axis_name=axis_key,
+                split_axis=0,
+                concat_axis=0,
+            ),
+            axis=axis_no,
+        )
+
+    right = drive_the_racks(pair, CHIPS, 1)
     scale = lax.dynamic_slice_in_dim(cycle_sizes, me * owned + core * half, half).astype(
         jnp.float32
     )

time: 595 us -> 500 us (0.84)
  waiting for transfers between devices: 386 us -> 277 us
  local copies, waits for them, and re-layouts: 83.7 us -> 105 us
  between operations: 37.4 us -> 24.6 us
  starting transfers between devices: 14.9 us -> 21.8 us
    all_gather x1 -> x0, waiting for transfers between devices: 365 us -> none  [per_device(): right = lax.all_gather(pair, CHIPS, axis=1, tiled=True)]
    all_to_all x0 -> x1, waiting for transfers between devices: none -> 256 us  [drive_the_racks(): lax.all_to_all(jnp.stack(lax.axis_size(axis_key) * [payload], axis=0), ax...]
    reshape x0 -> x1, local copies, waits for them, and re-layouts: none -> 12.7 us  [drive_the_racks(): jnp.concatenate(lax.all_to_all(jnp.stack(lax.axis_size(axis_key) * [paylo...]
    another operation x1 -> x2, local copies, waits for them, and re-layouts: 0.74 us -> 9.73 us  [the longest x1 8.98 us: drive_the_racks(): jnp.stack(lax.axis_size(axis_key) * [payload], axis=0)]
    all_to_all x0 -> x1, starting transfers between devices: none -> 6.47 us  [drive_the_racks(): lax.all_to_all(jnp.stack(lax.axis_size(axis_key) * [payload], axis=0), ax...]
  transfers between devices with their start and end apart: 6 -> 6, of which waited for: 5 -> 5; matrix products, arithmetic and copies ran while one was open for 3% -> 4% of each run, Pallas kernels for 0% -> 0%
where the time goes in v1:
time: 500 us; the launch traced here: 498 us
  waiting for transfers between devices  277 us (55%)
  local copies, waits for them, and re-layouts  105 us (21%)
  other arithmetic  40.1 us (8%)
  matrix products  30.1 us (6%)
  between operations  24.6 us (5%)
  starting transfers between devices  21.8 us (4%)
    all_to_all x1, waiting for transfers between devices, drive_the_racks(): lax.all_to_all(jnp.stack(lax.axis_size(axis_key) * [payload], axis=0), ax...  256 us
    gather x1, local copies, waits for them, and re-layouts, per_device(): ordered = jnp.take(block.T, pixel_order, axis=0)  44.1 us
    dot_general x2, matrix products, correlate(): jnp.einsum('rfs,rgs->rfg', left, right, precision=lax.Precision.HIGH, pre...  30.1 us
    dynamic_slice x9, local copies, waits for them, and re-layouts, per_device(): lax.dynamic_slice_in_dim(ordered, starts[d * owned], window, 0)  21.8 us
    select_n x1, other arithmetic, per_device(): jnp.where(core == 0, jnp.concatenate([mine, back], 0), jnp.concatenate([b...  15.7 us
    all_to_all x1, waiting for transfers between devices, per_device(): got = lax.all_to_all(chunks, PIX, 0, 0, tiled=True)  14.7 us
    unnamed x32, local copies, waits for them, and re-layouts  13.4 us
    reshape x1, local copies, waits for them, and re-layouts, drive_the_racks(): jnp.concatenate(lax.all_to_all(jnp.stack(lax.axis_size(axis_key) * [paylo...  12.7 us
  transfers between devices with their start and end apart: 6, of which 5 were waited for; matrix products, arithmetic and copies ran while one was open for 4% of the time, Pallas kernels for 0%

profile of v1, /device:TPU:1, one launch (start us, length us, event | category | flops | bytes accessed | tf_op | source)
XLA Modules:
  0.0 498.5 jit_solution(17329274964172509540)
XLA Ops:
  1.6 1.7 fusion.42
  15.0 4.9 copy.26
  24.8 44.1 %gather_fusion = f32[12288,24]{1,0:T(8,128)} fusion(f32[12288,24]{1,0:T(8,128)} %bitcast.93, s32[12288]{0:T(1024)S(1)} %fusion.39), kind=kCustom, calls=%fused_computation | custom fusion | bytes 2408448 | tf_op jit(solution)/shard_map/jit(_take)/gather | solution.py:44
  68.9 8.6 %broadcast_select_fusion = f32[12288,24]{1,0:T(8,128)S(1)} fusion(f32[12288,24]{1,0:T(8,128)} %gather_fusion, pred[12288]{0:T(1024)(128)(4,1)S(1)} %compare_and_fusion), kind=kLoop, calls=%fused_computation.10 | loop fusion | flops 294912 | bytes 2371584 | tf_op jit(solution)/shard_map/jit(_take)/select_n | solution.py:44
  77.5 7.3 %pad_dynamic-slice_fusion = (f32[3072,24]{1,0:T(8,128)}, f32[3072,24]{1,0:T(8,128)}, f32[3072,24]{1,0:T(8,128)}, f32[3072,24]{1,0:T(8,128)}, f32[3072,24]{1,0:T(...) fusion(s32[]{:T(128)S(6)} %select_n.151, f32[12288,24]{1,0:T(8,128)S(1)} %broadcast_select_fusion, ...), kind=kLoop, calls=%fused_computation.2 | loop fusion | bytes 3538976 | tf_op jit(solution)/shard_map/dynamic_slice | solution.py:47
  84.8 2.0 copy.35
  86.8 2.6 copy.29
  91.7 2.7 copy.32
  94.4 2.6 copy.33
  107.1 8.5 %all-to-all-start = ((f32[8,3072,24]{1,2,0:T(8,128)}), f32[8,3072,24]{1,2,0:T(8,128)S(1)}, u32[]{:S(2)}, u32[]{:S(2)}) async-start(f32[8,3072,24]{1,2,0:T(8,128)} %bitcast_dynamic-update-slice_fusion), calls=%async_computation | async-start | bytes 4718592 | tf_op jit(solution)/shard_map/all_to_all | solution.py:49
  129.9 14.7 %all-to-all-done = f32[8,3072,24]{1,2,0:T(8,128)S(1)} async-done(((f32[8,3072,24]{1,2,0:T(8,128)}), f32[8,3072,24]{1,2,0:T(8,128)S(1)}, u32[]{:S(2)}, u32[]{:S(2)}) %all-to-all-start) | async-done | bytes 2359328 | tf_op jit(solution)/shard_map/all_to_all | solution.py:49
  147.5 2.0 bitcast_divide_fusion
  149.5 3.4 collective-permute-start
  152.9 1.9 collective-permute-start.1
  155.5 2.5 collective-permute-done.1
  158.0 4.7 fusion.3
  163.2 2.8 collective-permute-done.2
  166.2 9.0 %stack.83 = f32[8,4,384,384]{3,2,1,0:T(8,128)} broadcast(f32[4,384,384]{2,1,0:T(8,128)S(1)} %maximum_select_fusion.1), dimensions={1,2,3} | broadcast | bytes 21233664 | tf_op jit(solution)/shard_map/stack | solution.py:79
  175.2 6.5 %all-to-all-start.1 = ((f32[8,4,384,384]{3,2,1,0:T(8,128)}), f32[8,4,384,384]{3,2,1,0:T(8,128)}, u32[]{:S(2)}, u32[]{:S(2)}) async-start(f32[8,4,384,384]{3,2,1,0:T(8,128)} %stack.83), calls=%async_computation.1 | async-start | bytes 37748736 | tf_op jit(solution)/shard_map/all_to_all | solution.py:78
  181.8 255.8 %all-to-all-done.1 = f32[8,4,384,384]{3,2,1,0:T(8,128)} async-done(((f32[8,4,384,384]{3,2,1,0:T(8,128)}), f32[8,4,384,384]{3,2,1,0:T(8,128)}, u32[]{:S(2)}, u32[]{:S(2)}) %all-to-all-start.1) | async-done | bytes 18874400 | tf_op jit(solution)/shard_map/all_to_all | solution.py:78
  437.6 12.7 %copy.36 = f32[4,8,384,384]{3,2,1,0:T(8,128)} copy(f32[4,8,384,384]{3,2,0,1:T(8,128)} %bitcast.51) | data formatting | bytes 37748736 | tf_op jit(solution)/shard_map/reshape | solution.py:77
  450.3 16.5 %fusion.10 = f32[4,192,3072]{2,1,0:T(8,128)} fusion(f32[4,3072,384]{2,1,0:T(8,128)} %bitcast.94, f32[4,192,384]{2,1,0:T(8,128)S(1)} %collective-permute-done.2, f32[4]{0:T(128)S(1)} %dynamic-slice_convert_fusion), kind=kOutput, calls=%fused_computation.37 | convolution fusion | flops 5436112896 | bytes 29491216 | tf_op jit(solution)/shard_map/rfs,rgs->rfg/dot_general | solution.py:24
  468.1 13.6 %fusion.12 = f32[4,192,3072]{2,1,0:T(8,128)S(1)} fusion(f32[4,3072,384]{2,1,0:T(8,128)} %bitcast.95, f32[4,192,384]{2,1,0:T(8,128)S(1)} %get-tuple-element.13, f32[4]{0:T(128)S(1)} %dynamic-slice_convert_fusion), kind=kOutput, calls=%fused_computation.40 | convolution fusion | flops 5436112896 | bytes 29491216 | tf_op jit(solution)/shard_map/rfs,rgs->rfg/dot_general | solution.py:24
  482.7 15.7 %maximum_select_fusion = f32[8,192,3072]{2,1,0:T(8,128)} fusion(f32[4,192,3072]{2,1,0:T(8,128)} %collective-permute-done.3, f32[4,192,3072]{2,1,0:T(8,128)S(1)} %fusion.12, pred[]{:T(512)S(6)} %eq.4), kind=kLoop, calls=%fused_computation.1 | loop fusion | flops 14155776 | bytes 37748736 | tf_op jit(solution)/shard_map/jit(_where)/select_n | solution.py:95
  (69 shorter events, 27.2 us)
Async XLA Ops:
  84.8 4.6 copy-start.4
  84.8 5.8 %copy-start.3 = (f32[3072,24]{1,0:T(8,128)S(1)}, f32[3072,24]{1,0:T(8,128)}, u32[]{:S(2)}) copy-start(f32[3072,24]{1,0:T(8,128)} %get-tuple-element.8) | copy-start | bytes 884740
  90.5 6.4 %copy-start.2 = (f32[3072,24]{1,0:T(8,128)S(1)}, f32[3072,24]{1,0:T(8,128)}, u32[]{:S(2)}) copy-start(f32[3072,24]{1,0:T(8,128)} %get-tuple-element.11) | copy-start | bytes 884740
  91.7 6.4 %copy-start.1 = (f32[3072,24]{1,0:T(8,128)S(1)}, f32[3072,24]{1,0:T(8,128)}, u32[]{:S(2)}) copy-start(f32[3072,24]{1,0:T(8,128)} %get-tuple-element.12) | copy-start | bytes 884740
  98.1 4.6 copy-start.9
  98.1 5.3 %copy-start.8 = (f32[3072,24]{0,1:T(8,128)S(1)}, f32[3072,24]{0,1:T(8,128)}, u32[]{:S(2)}) copy-start(f32[3072,24]{0,1:T(8,128)} %copy.31) | copy-start | bytes 884740
  98.1 6.1 %copy-start.7 = (f32[3072,24]{0,1:T(8,128)S(1)}, f32[3072,24]{0,1:T(8,128)}, u32[]{:S(2)}) copy-start(f32[3072,24]{0,1:T(8,128)} %copy.32) | copy-start | bytes 884740
  98.1 6.8 %copy-start.6 = (f32[3072,24]{0,1:T(8,128)S(1)}, f32[3072,24]{0,1:T(8,128)}, u32[]{:S(2)}) copy-start(f32[3072,24]{0,1:T(8,128)} %copy.33) | copy-start | bytes 884740
  98.1 7.5 %copy-start.5 = (f32[3072,24]{0,1:T(8,128)S(1)}, f32[3072,24]{0,1:T(8,128)}, u32[]{:S(2)}) copy-start(f32[3072,24]{0,1:T(8,128)} %copy.34) | copy-start | bytes 884740
  107.1 37.5 %all-to-all-start = ((f32[8,3072,24]{1,2,0:T(8,128)}), f32[8,3072,24]{1,2,0:T(8,128)S(1)}, u32[]{:S(2)}, u32[]{:S(2)}) async-start(f32[8,3072,24]{1,2,0:T(8,128)} %bitcast_dynamic-update-slice_fusion), calls=%async_computation | async-start | bytes 4718592 | tf_op jit(solution)/shard_map/all_to_all | solution.py:49
  145.8 1.4 copy-start
  147.5 7.3 %copy-start.11 = (f32[5]{0:T(128)S(1)}, f32[5]{0:T(128)}, u32[]{:S(2)}) copy-start(f32[5]{0:T(128)} %param.7) | copy-start | bytes 64
  149.5 6.0 %collective-permute-start = (f32[8,384,2]{1,2,0:T(2,128)S(1)}, f32[8,384,2]{1,2,0:T(2,128)S(1)}, u32[]{:S(2)}, u32[]{:S(2)}) collective-permute-start(f32[8,384,2]{1,2,0:T(2,128)S(1)} %get-tuple-element.15), channel_id=1, source_target_pairs={{0,1},{1,2},{2,3},{3,4},{4,5},{5,6},{6,7},{7,8},{8,9},{9,10},{10,1... | collective-permute-start | bytes 73736 | tf_op jit(solution)/shard_map/ppermute | solution.py:18
  152.9 5.1 %collective-permute-start.1 = (f32[8,384,2]{1,2,0:T(2,128)S(1)}, f32[8,384,2]{1,2,0:T(2,128)S(1)}, u32[]{:S(2)}, u32[]{:S(2)}) collective-permute-start(f32[8,384,2]{1,2,0:T(2,128)S(1)} %get-tuple-element.16), channel_id=1, source_target_pairs={{1,0},{2,1},{3,2},{4,3},{5,4},{6,5},{7,6},{8,7},{9,8},{10,9},{11,1... | collective-permute-start | bytes 73736 | tf_op jit(solution)/shard_map/ppermute | solution.py:19
  163.0 3.1 collective-permute-start.2
  175.2 6.5 %copy-start.10 = (s32[64]{0:T(128)S(1)}, s32[64]{0:T(128)}, u32[]{:S(2)}) copy-start(s32[64]{0:T(128)} %param.6) | copy-start | bytes 772
  175.2 262.4 %all-to-all-start.1 = ((f32[8,4,384,384]{3,2,1,0:T(8,128)}), f32[8,4,384,384]{3,2,1,0:T(8,128)}, u32[]{:S(2)}, u32[]{:S(2)}) async-start(f32[8,4,384,384]{3,2,1,0:T(8,128)} %stack.83), calls=%async_computation.1 | async-start | bytes 37748736 | tf_op jit(solution)/shard_map/all_to_all | solution.py:78
  466.8 15.9 %collective-permute-start.3 = (f32[4,192,3072]{2,1,0:T(8,128)}, f32[4,192,3072]{2,1,0:T(8,128)}, u32[]{:S(2)}, u32[]{:S(2)}) collective-permute-start(f32[4,192,3072]{2,1,0:T(8,128)} %fusion.10), channel_id=1, source_target_pairs={{0,1},{1,0},{2,3},{3,2},{4,5},{5,4},{6,7},{7,6},{8,9},{9,8},{10,11... | collective-permute-start | bytes 28311560 | tf_op jit(solution)/shard_map/ppermute | solution.py:93
